TPU v7x, 256 devices: a whole 4x4x8 slice. The times are simulated.
256 devices in a mesh: row: 8 (over z), col: 32 (over y, x, core).
Axes of the slice: x: 4, y: 4, z: 8, core: 2. Of those that a mesh axis runs over, the one named last changes fastest.
Arguments:
- hidden_in: bfloat16 [1024, 2304], P('row', 'col'), may hold values from -40 to 40
- attn_gain: float32 [2304], P('col'), may hold values from 0.1 to 1.9
- qkv_weight: bfloat16 [2304, 6912], P('col'), may hold values from -0.125 to 0.125
- out_weight: bfloat16 [2304, 2304], P(None, 'col'), may hold values from -0.125 to 0.125
- moe_gain: float32 [2304], P('col'), may hold values from 0.1 to 1.9
- router_weight: float32 [2304, 8], P('col'), may hold values from -0.125 to 0.125
- expert_gate: bfloat16 [8, 2304, 5760], P('row', None, 'col'), may hold values from -0.125 to 0.125
- expert_up: bfloat16 [8, 2304, 5760], P('row', None, 'col'), may hold values from -0.125 to 0.125
- expert_down: bfloat16 [8, 5760, 2304], P('row', 'col'), may hold values from -0.078125 to 0.078125
- cache_keys: bfloat16 [2048, 64, 2304], P(('row', 'col')), may hold values from -400 to 400
- cache_values: bfloat16 [2048, 64, 2304], P(('row', 'col')), may hold values from -12 to 12
- block_table: int32 [8, 4, 64], P('row'), may hold values from 0 to 2047, as said below
- prefix_lengths: int32 [8, 4], P('row'), may hold values from 1024 to 4096, as said below
- prompt_lengths: int32 [8, 4], P('row'), may hold values from 1 to 64, 128 in all within a row
- routed_experts: int32 [1024, 2], P('row'), may hold values from 0 to 7, all different within a row; in each aligned block of 128 rows (0 to 127, 128 to 255, ...) at most 64 rows name the same one
Outputs:
- attn_out: bfloat16 [1024, 2304], P('row', 'col')
- moe_out: bfloat16 [1024, 2304], P('row', 'col')
- layer_out: bfloat16 [1024, 2304], P('row', 'col')
Inputs may be any that keep to these rules, and one draw needn't show every extreme that they name: `block_table`: entry [g, q, j] lies among the 8 pages that begin at (g * 32 + j % 32) * 8; the entries that fall among the same 8 pages are distinct. `prefix_lengths`: some request has exactly 4096 cached tokens. `prompt_lengths`: the 4 lengths of a group sum to 128; the longest of each group is exactly 64. `routed_experts`: the 2 experts of a token differ; among the tokens of one group no expert is named more than 64 times, and in some group an expert reaches 64; every expert is named by some token.
All inputs are finite; a program needn't handle non-finite values.
Results may differ from a plain program's by a relative error of at most 0.02.
The roundings to bfloat16 on the way count: a program that leaves them out, or rounds other values in their place, can miss the bound.
Values may be sent and summed in bfloat16 or wider, within the bound.
No kernel may reach another device: no remote copies, remote signals or barrier semaphores. Data moves between devices by JAX's collectives and lax.ppermute only.
A program may use at most 192 MiB of HBM per device.

v0:
```python
import math
import jax
import jax.numpy as jnp
from jax import lax
from jax.sharding import PartitionSpec as P

D = 2304
HEAD_DIM = 64
TOP = 2
norm_epsilon = 1e-05
residual_scale = 1.4 / math.sqrt(40.0)
rotary_base = 10000.0
masked_score = -1e30


def merged(value, axis, join):
    pieces = jax.tree.map(lambda part: lax.all_gather(part, axis), value)
    head = jax.tree.map(lambda part: part[0], pieces)
    tail = jax.tree.map(lambda part: part[1:], pieces)
    running, _ = lax.scan(lambda running, slab: (join(running, slab), None), head, tail)
    return running


def rotate(values, positions, head_dim):
    row_count = values.shape[0]
    head_count = values.shape[1] // head_dim
    half_dim = head_dim // 2
    frequency = rotary_base ** (-2.0 * jnp.arange(half_dim, dtype=jnp.float32) / head_dim)
    angles = positions.astype(jnp.float32)[:, None] * frequency[None, :]
    cosine = jnp.cos(angles)[:, None, :]
    sine_part = jnp.sin(angles)[:, None, :]
    shaped = values.reshape(row_count, head_count, head_dim)
    first_half = shaped[:, :, :half_dim]
    second_half = shaped[:, :, half_dim:]
    turned = jnp.concatenate(
        [
            first_half * cosine - second_half * sine_part,
            second_half * cosine + first_half * sine_part,
        ],
        axis=2,
    )
    return turned.reshape(row_count, head_count * head_dim)


def token_layout(prompt_row, prefix_row, row_count):
    run_ends = jnp.cumsum(prompt_row, dtype=jnp.int32)
    starts = run_ends - prompt_row
    offsets = jnp.arange(row_count, dtype=jnp.int32)
    request = jnp.sum(
        (offsets[:, None] >= run_ends[None, :]).astype(jnp.int32), axis=1, dtype=jnp.int32
    )
    member = request[:, None] == jnp.arange(prompt_row.shape[0], dtype=jnp.int32)[None, :]
    start_of = jnp.sum(jnp.where(member, starts[None, :], 0), axis=1, dtype=jnp.int32)
    prefix_of = jnp.sum(jnp.where(member, prefix_row[None, :], 0), axis=1, dtype=jnp.int32)
    return (request, prefix_of + offsets - start_of)


def rescale(summed, factor):
    group_count, row_count, feature_width = summed.shape
    group_size = factor.shape[1]
    shaped = summed.reshape(group_count, row_count, group_size, feature_width // group_size)
    shaped = shaped * jnp.transpose(factor, (0, 2, 1))[:, :, :, None]
    return shaped.reshape(group_count, row_count, feature_width)


def divide_rows(summed, total_weight):
    group_count, row_count, feature_width = summed.shape
    group_size = total_weight.shape[1]
    shaped = summed.reshape(group_count, row_count, group_size, feature_width // group_size)
    shaped = shaped / jnp.transpose(total_weight, (0, 2, 1))[:, :, :, None]
    return shaped.reshape(group_count, row_count, feature_width)


def combine_parts(earlier_part, later_part):
    largest = jnp.maximum(earlier_part[0], later_part[0])
    factor_one = jnp.exp(earlier_part[0] - largest)
    factor_two = jnp.exp(later_part[0] - largest)
    total_weight = earlier_part[1] * factor_one + later_part[1] * factor_two
    summed = rescale(earlier_part[2], factor_one) + rescale(later_part[2], factor_two)
    return (largest, total_weight, summed)


def on_device(
    hidden_in,
    attn_gain,
    qkv_weight,
    out_weight,
    moe_gain,
    router_weight,
    expert_gate,
    expert_up,
    expert_down,
    cache_keys,
    cache_values,
    block_table,
    prefix_lengths,
    prompt_lengths,
    routed_experts,
):
    col_count = lax.axis_size("col")
    row_devices = lax.axis_size("row")
    col_index = lax.axis_index("col")
    row_index = lax.axis_index("row")
    tok_rows = hidden_in.shape[0]
    feature_width = hidden_in.shape[1]
    head_total = out_weight.shape[0]
    head_count = head_total // HEAD_DIM
    key_share = tok_rows // col_count
    request, position = token_layout(prompt_lengths[0], prefix_lengths[0], tok_rows)
    own_start = col_index * key_share
    key_position = lax.dynamic_slice_in_dim(position, own_start, key_share)
    key_request = lax.dynamic_slice_in_dim(request, own_start, key_share)
    residual = hidden_in.astype(jnp.float32)
    squares = lax.psum(jnp.sum(residual * residual, axis=1), "col")
    scale_one = lax.rsqrt(squares / D + norm_epsilon)
    normed = (residual * scale_one[:, None] * attn_gain[None, :]).astype(jnp.bfloat16)
    query_part = jnp.dot(normed, qkv_weight[:, :head_total], preferred_element_type=jnp.float32)
    query_sum = lax.psum(query_part, "col")
    queries = (rotate(query_sum, position, HEAD_DIM) * HEAD_DIM ** (-0.5)).astype(jnp.bfloat16)
    key_value = lax.psum_scatter(
        jnp.dot(normed, qkv_weight[:, head_total:], preferred_element_type=jnp.float32).astype(
            jnp.bfloat16
        ),
        "col",
        scatter_dimension=0,
        tiled=True,
    ).astype(jnp.float32)
    new_keys = rotate(key_value[:, :head_total], key_position, HEAD_DIM).astype(jnp.bfloat16)
    new_values = key_value[:, head_total:].astype(jnp.bfloat16)
    pool_size = cache_keys.shape[0]
    page_size = cache_keys.shape[1]
    req_count = block_table.shape[1]
    pages_each = block_table.shape[2] // col_count
    page_table = block_table[0].reshape(req_count, pages_each, col_count)
    own_pages = lax.dynamic_slice_in_dim(page_table, col_index, 1, 2).reshape(
        req_count * pages_each
    )
    pool_offset_begin = (row_index * col_count + col_index) * pool_size
    slot_ids = jnp.arange(pool_size, dtype=jnp.int32)
    entry_ids = jnp.arange(req_count * pages_each, dtype=jnp.int32)
    slot_match = (own_pages - pool_offset_begin)[None, :] == slot_ids[:, None]
    entry_request = entry_ids // pages_each
    entry_page = entry_ids % pages_each * col_count + col_index
    slot_request = jnp.sum(
        jnp.where(slot_match, entry_request[None, :], 0), axis=1, dtype=jnp.int32
    )
    slot_page = jnp.sum(jnp.where(slot_match, entry_page[None, :], 0), axis=1, dtype=jnp.int32)
    prefix_row = prefix_lengths[0]
    slot_prefix = jnp.sum(
        jnp.where(
            slot_request[:, None] == jnp.arange(req_count, dtype=jnp.int32)[None, :],
            prefix_row[None, :],
            0,
        ),
        axis=1,
        dtype=jnp.int32,
    )
    cache_position = (
        slot_page[:, None] * page_size + jnp.arange(page_size, dtype=jnp.int32)[None, :]
    )
    cache_live = (
        (cache_position < slot_prefix[:, None]).astype(jnp.int32).reshape(pool_size * page_size)
    )
    cache_request = jnp.broadcast_to(slot_request[:, None], (pool_size, page_size)).reshape(
        pool_size * page_size
    )
    cache_mask = (request[:, None] == cache_request[None, :]) & (cache_live[None, :] > 0)
    fresh_mask = (request[:, None] == key_request[None, :]) & (
        key_position[None, :] <= position[:, None]
    )
    group_size = math.gcd(head_count, 4)
    group_count = head_count // group_size
    query_heads = queries.reshape(tok_rows, head_count, HEAD_DIM)
    cached_key_heads = cache_keys.reshape(pool_size * page_size, head_count, HEAD_DIM)
    cached_value_heads = cache_values.reshape(pool_size * page_size, head_count, HEAD_DIM)
    fresh_key_heads = new_keys.reshape(key_share, head_count, HEAD_DIM)
    fresh_value_heads = new_values.reshape(key_share, head_count, HEAD_DIM)

    def head_group(group_index):
        first_head = group_index * group_size
        query_piece = lax.dynamic_slice_in_dim(query_heads, first_head, group_size, 1)
        key_piece = lax.dynamic_slice_in_dim(cached_key_heads, first_head, group_size, 1)
        value_piece = lax.dynamic_slice_in_dim(cached_value_heads, first_head, group_size, 1)
        fresh_key_piece = lax.dynamic_slice_in_dim(fresh_key_heads, first_head, group_size, 1)
        fresh_value_piece = lax.dynamic_slice_in_dim(fresh_value_heads, first_head, group_size, 1)
        score_matrix = jnp.einsum(
            "thd,khd->htk", query_piece, key_piece, preferred_element_type=jnp.float32
        )
        score_matrix = jnp.where(cache_mask[None], score_matrix, masked_score)
        fresh_scores = jnp.einsum(
            "thd,khd->htk", query_piece, fresh_key_piece, preferred_element_type=jnp.float32
        )
        fresh_scores = jnp.where(fresh_mask[None], fresh_scores, masked_score)
        largest = jnp.maximum(jnp.max(score_matrix, axis=2), jnp.max(fresh_scores, axis=2))
        cached_exp = jnp.where(cache_mask[None], jnp.exp(score_matrix - largest[:, :, None]), 0.0)
        fresh_exp = jnp.where(fresh_mask[None], jnp.exp(fresh_scores - largest[:, :, None]), 0.0)
        total_weight = jnp.sum(cached_exp, axis=2) + jnp.sum(fresh_exp, axis=2)
        summed = jnp.einsum(
            "htk,khd->thd",
            cached_exp.astype(jnp.bfloat16),
            value_piece,
            preferred_element_type=jnp.float32,
        )
        summed = summed + jnp.einsum(
            "htk,khd->thd",
            fresh_exp.astype(jnp.bfloat16),
            fresh_value_piece,
            preferred_element_type=jnp.float32,
        )
        return (largest, total_weight, summed.reshape(tok_rows, group_size * HEAD_DIM))

    largest, total_weight, summed = lax.map(head_group, jnp.arange(group_count, dtype=jnp.int32))
    largest, total_weight, summed = merged((largest, total_weight, summed), "col", combine_parts)
    attended = divide_rows(summed, total_weight).astype(jnp.bfloat16)
    projected = jnp.einsum(
        "gtx,gxo->to",
        attended,
        out_weight.reshape(group_count, group_size * HEAD_DIM, feature_width),
        preferred_element_type=jnp.float32,
    )
    attn_out = projected.astype(jnp.bfloat16)
    middle = (residual + residual_scale * attn_out.astype(jnp.float32)).astype(jnp.bfloat16)
    middle_wide = middle.astype(jnp.float32)
    squares_two = lax.psum(jnp.sum(middle_wide * middle_wide, axis=1), "col")
    scale_two = lax.rsqrt(squares_two / D + norm_epsilon)
    moe_normed_f = middle_wide * scale_two[:, None] * moe_gain[None, :]
    logits = lax.psum(jnp.dot(moe_normed_f, router_weight, precision=lax.Precision.HIGHEST), "col")
    moe_normed = moe_normed_f.astype(jnp.bfloat16)
    expert_local = expert_gate.shape[0]
    expert_total = expert_local * row_devices
    capacity = 2 * TOP * tok_rows // expert_total
    onehot_three = (
        routed_experts[:, :, None] == jnp.arange(expert_total, dtype=jnp.int32)[None, None, :]
    )
    selected_logits = jnp.sum(jnp.where(onehot_three, logits[:, None, :], 0.0), axis=2)
    first_gate = jax.nn.sigmoid(selected_logits[:, 0] - selected_logits[:, 1])
    gate_pair = jnp.stack([first_gate, 1.0 - first_gate], axis=1)
    onehot = onehot_three.astype(jnp.int32).reshape(tok_rows * TOP, expert_total)
    earlier = jnp.cumsum(onehot, axis=0, dtype=jnp.int32) - onehot
    slot_index = jnp.sum(earlier * onehot, axis=1, dtype=jnp.int32)
    target = routed_experts.reshape(tok_rows * TOP) * capacity + slot_index
    token_local = jnp.arange(tok_rows * TOP, dtype=jnp.int32) // TOP
    source = jnp.zeros((expert_total * capacity,), jnp.int32).at[target].set(token_local)
    filled = jnp.zeros((expert_total * capacity,), jnp.int32).at[target].set(1)
    outgoing = jnp.where(
        filled[:, None] > 0, moe_normed[source], jnp.zeros((), jnp.bfloat16)
    ).reshape(expert_total, capacity, feature_width)
    arrived = lax.all_to_all(outgoing, "row", split_axis=0, concat_axis=0, tiled=True)
    expert_rows = (
        arrived.reshape(row_devices, expert_local, capacity, feature_width)
        .transpose(1, 0, 2, 3)
        .reshape(expert_local, row_devices * capacity, feature_width)
    )
    feature_piece = lax.all_gather(expert_rows, "col", axis=2, tiled=True)
    gate_next = jnp.einsum(
        "erd,edf->erf", feature_piece, expert_gate, preferred_element_type=jnp.float32
    )
    up_next = jnp.einsum(
        "erd,edf->erf", feature_piece, expert_up, preferred_element_type=jnp.float32
    )
    hidden = (jax.nn.silu(gate_next) * up_next).astype(jnp.bfloat16)
    received_rows = hidden.shape[1]
    value_partial_sum = jnp.einsum(
        "efo,erf->oer", expert_down, hidden, preferred_element_type=jnp.float32
    )
    expert_out = lax.psum_scatter(
        value_partial_sum.reshape(
            lax.axis_size("col") * feature_width, expert_local * received_rows
        ).astype(jnp.bfloat16),
        "col",
        scatter_dimension=0,
        tiled=True,
    )
    returned = lax.all_to_all(
        expert_out.reshape(feature_width, expert_local, received_rows),
        "row",
        split_axis=2,
        concat_axis=1,
        tiled=True,
    )
    flat_back = returned.reshape(feature_width, expert_total * capacity)
    picked = (
        jnp.take(flat_back, target, axis=1)
        .astype(jnp.float32)
        .reshape(feature_width, tok_rows, TOP)
    )
    moe_columns = jnp.sum(picked * gate_pair[None, :, :], axis=2).astype(jnp.bfloat16)
    moe_out = moe_columns.T
    layer_out = (middle_wide + residual_scale * moe_out.astype(jnp.float32)).astype(jnp.bfloat16)
    return (attn_out, moe_out, layer_out)


def solution(mesh):
    in_specs = (
        P("row", "col"),
        P("col"),
        P("col", None),
        P(None, "col"),
        P("col"),
        P("col", None),
        P("row", None, "col"),
        P("row", None, "col"),
        P("row", "col", None),
        P(("row", "col"), None, None),
        P(("row", "col"), None, None),
        P("row", None, None),
        P("row", None),
        P("row", None),
        P("row", None),
    )
    out_specs = (P("row", "col"), P("row", "col"), P("row", "col"))
    return jax.shard_map(
        on_device, mesh=mesh, in_specs=in_specs, out_specs=out_specs, check_vma=False
    )
```

profile of v0, /device:TPU:2, one launch (start us, length us, event | category | flops | bytes accessed | tf_op | source)
XLA Modules:
  0.0 942.3 jit_solution(6926186442801343392)
XLA Ops:
  8.0 62.3 %psum.28 = f32[128]{0:T(128)S(1)} all-reduce(f32[128]{0:T(128)S(1)} %fusion.64), channel_id=1, replica_groups=mesh['row'=8,'col'=32] {'col'}, use_global_device_ids=true, to_apply=%region_1.2 | all-reduce | flops 128 | bytes 1024 | tf_op jit(solution)/shard_map/psum | solution.py:114
  70.3 2.7 convolution_convert_fusion
  77.7 5.0 reshape.454
  82.7 6.9 copy.162
  89.5 5.0 reshape.455
  94.5 6.7 copy.163
  102.5 88.4 %all-reduce.6.cloned.1.call-done = bf16[128,4608]{1,0:T(8,128)(2,1)} async-done(((bf16[128,4608]{1,0:T(8,128)(2,1)}), bf16[128,4608]{1,0:T(8,128)(2,1)}) %all-reduce.6.cloned.1.call-update) | async-done | bytes 1179664
  192.2 117.1 %all-reduce.4.cloned.1.call-done = f32[128,36,64]{0,2,1:T(8,128)} async-done(((f32[128,36,64]{0,2,1:T(8,128)}), f32[128,36,64]{0,2,1:T(8,128)}) %all-reduce.4.cloned.1.call-update) | async-done | bytes 1179664 | tf_op jit(solution)/shard_map/psum | solution.py:118
  310.9 51.9 %while.31 = (s32[]{:T(128)}, f32[9,4,128]{2,1,0:T(4,128)S(1)}, f32[9,4,128]{2,1,0:T(4,128)S(1)}, f32[9,128,256]{2,1,0:T(8,128)}, s32[9]{0:T(128)S(1)}, /*index=5...) while((s32[]{:T(128)}, f32[9,4,128]{2,1,0:T(4,128)S(1)}, ...), condition=%wide.region_16.17_spmd.clone.clone, body=%wide.region_11.16_spmd.clone.clone.sunk | while | flops 69911040 | bytes 5058339 | solution.py:212
  368.0 24.4 %all-gather = f32[288,4,128]{2,1,0:T(4,128)S(1)} all-gather(f32[9,4,128]{2,1,0:T(4,128)S(1)} %get-tuple-element.105), channel_id=2, replica_groups=mesh['row'=8,'col'=32] {'col'}, dimensions={0}, use_global_device_ids=true | all-gather | bytes 608256 | tf_op jit(solution)/shard_map/all_gather | solution.py:17
  392.5 25.6 %all-gather.1 = f32[288,4,128]{2,1,0:T(4,128)S(1)} all-gather(f32[9,4,128]{2,1,0:T(4,128)S(1)} %get-tuple-element.106), channel_id=3, replica_groups=mesh['row'=8,'col'=32] {'col'}, dimensions={0}, use_global_device_ids=true | all-gather | bytes 608256 | tf_op jit(solution)/shard_map/all_gather | solution.py:17
  418.2 76.0 %all-gather.8.cloned.1.call-done = f32[288,128,256]{2,1,0:T(8,128)} async-done(((f32[9,128,256]{2,1,0:T(8,128)}), f32[288,128,256]{2,1,0:T(8,128)}) %all-gather.8.cloned.1.call-update) | async-done | bytes 37748752 | tf_op jit(solution)/shard_map/all_gather | solution.py:17
  496.8 26.9 %slice.93 = f32[279,128,256]{2,1,0:T(8,128)} slice(f32[288,128,256]{2,1,0:T(8,128)} %all-gather.8.cloned.1.call-done), slice={[9:288], [0:128], [0:256]} | slice | bytes 73138176 | tf_op jit(solution)/shard_map/slice | solution.py:19
  523.7 168.2 %while.30 = (s32[]{:T(128)}, f32[9,4,128]{2,1,0:T(4,128)S(1)}, f32[9,4,128]{2,1,0:T(4,128)S(1)}, f32[9,128,256]{1,2,0:T(8,128)}, f32[31,9,4,128]{3,2,1,0:T(4,128...) while((s32[]{:T(128)}, f32[9,4,128]{2,1,0:T(4,128)S(1)}, ...), condition=%wide.region_18.19_spmd, body=%wide.region_17.18_spmd.sunk | while | flops 916994 | bytes 17676496 | solution.py:20
  531.9 2.6 fusion.111
  694.2 60.6 %psum.30 = f32[128]{0:T(128)S(1)} all-reduce(f32[128]{0:T(128)S(1)} %get-tuple-element.401), channel_id=1, replica_groups=mesh['row'=8,'col'=32] {'col'}, use_global_device_ids=true, to_apply=%region_24.25 | all-reduce | flops 128 | bytes 1024 | tf_op jit(solution)/shard_map/psum | solution.py:224
  756.5 15.9 %all_to_all.14 = bf16[8,64,72]{2,1,0:T(8,128)(2,1)S(1)} all-to-all(bf16[8,64,72]{2,1,0:T(8,128)(2,1)S(1)} %broadcast_select_fusion), channel_id=1, replica_groups=mesh['row'=8,'col'=32] {'row'}, dimensions={0} | all-to-all | bytes 147456 | tf_op jit(solution)/shard_map/all_to_all | solution.py:248
  773.2 44.9 %all-gather.6.cloned.1.call-done = bf16[1,512,2304]{1,2,0:T(8,128)(2,1)} async-done(((bf16[1,512,72]{1,2,0:T(8,128)(2,1)}), bf16[1,512,2304]{1,2,0:T(8,128)(2,1)}) %all-gather.6.cloned.1.call-update) | async-done | bytes 2359312 | tf_op jit(solution)/shard_map/all_gather | solution.py:254
  818.1 3.0 fusion.36
  821.2 3.4 fusion.33
  827.9 60.4 %psum.31 = f32[128,8]{0,1:T(8,128)S(1)} all-reduce(f32[128,8]{0,1:T(8,128)S(1)} %fusion.70), channel_id=1, replica_groups=mesh['row'=8,'col'=32] {'col'}, use_global_device_ids=true, to_apply=%region_27.28 | all-reduce | flops 1024 | bytes 8192 | tf_op jit(solution)/shard_map/psum | solution.py:227
  888.4 25.3 %reduce-scatter.4.cloned.1.call-done = bf16[72,512]{1,0:T(8,128)(2,1)} async-done(((bf16[2304,512]{1,0:T(8,128)(2,1)}), bf16[72,512]{1,0:T(8,128)(2,1)}) %reduce-scatter.4.cloned.1.call-update) | async-done | bytes 73744
  917.8 7.0 all-to-all-start.1
  925.0 8.3 all-to-all-done.1
  (695 shorter events, 240.1 us)
Async XLA Ops:
  7.2 814.0 %copy-start = (bf16[1,180,2304]{2,1,0:T(8,128)(2,1)S(1)}, bf16[1,180,2304]{2,1,0:T(8,128)(2,1)}, u32[]{:S(2)}) copy-start(bf16[1,180,2304]{2,1,0:T(8,128)(2,1)} %param.27) | copy-start | bytes 2488324
  7.2 183.7 %all-reduce.6.cloned.1.call-start = ((), (), s32[]{:S(2)}) async-start(), calls=%async_computation.7 | async-start | bytes 2359296
  70.3 2.9 copy-start.8
  70.3 2.9 copy-start.12
  73.1 2.9 copy-start.17
  73.1 3.2 copy-start.14
  73.1 3.4 copy-start.11
  73.1 4.6 copy-start.1
  73.1 236.2 %all-reduce.4.cloned.1.call-start = ((), (), s32[]{:S(2)}) async-start(), calls=%async_computation.3 | async-start | bytes 2359296 | tf_op jit(solution)/shard_map/psum | solution.py:118
  75.8 418.3 %all-gather.8.cloned.1.call-start = ((), (), s32[]{:S(2)}) async-start(), calls=%async_computation.5 | async-start | bytes 38928384 | tf_op jit(solution)/shard_map/all_gather | solution.py:17
  82.7 6.9 copy-start.2
  94.5 6.7 copy-start.18
  362.8 455.3 %all-gather.6.cloned.1.call-start = ((), (), s32[]{:S(2)}) async-start(), calls=%async_computation.4 | async-start | bytes 2433024 | tf_op jit(solution)/shard_map/all_gather | solution.py:254
  526.5 2.6 copy-start.4
  531.9 2.6 copy-start.4
  537.3 2.6 copy-start.4
  542.8 2.6 copy-start.4
  548.2 2.6 copy-start.4
  553.6 2.6 copy-start.4
  651.3 2.6 copy-start.4
  691.9 62.9 %copy-start.13 = (f32[72]{0:T(128)S(1)}, f32[72]{0:T(128)}, u32[]{:S(2)}) copy-start(f32[72]{0:T(128)} %param.23) | copy-start | bytes 868
  694.2 123.9 %copy-start.15 = (bf16[1,2304,180]{1,2,0:T(8,128)(2,1)S(1)}, bf16[1,2304,180]{1,2,0:T(8,128)(2,1)}, u32[]{:S(2)}) copy-start(bf16[1,2304,180]{1,2,0:T(8,128)(2,1)} %param.25) | copy-start | bytes 2488324
  773.1 140.5 %reduce-scatter.4.cloned.1.call-start = ((), (), s32[]{:S(2)}) async-start(), calls=%async_computation.6 | async-start | bytes 2433024
  917.8 15.5 %all-to-all-start.1 = ((bf16[8,2,2304]{2,1,0:T(2,128)(2,1)}), bf16[8,2,2304]{2,1,0:T(2,128)(2,1)S(1)}, u32[]{:S(2)}, u32[]{:S(2)}) async-start(bf16[8,2,2304]{2,1,0:T(2,128)(2,1)} %reshape.465), calls=%async_computation.1 | async-start | bytes 147456 | tf_op jit(solution)/shard_map/all_to_all | solution.py:274
  (122 other events, 206.0 us)
Sparse Core Ops, SparseCore 0:
  73.2 117.6 all-reduce.5
  194.2 115.0 all-reduce.3
  362.9 131.1 all-gather.7
  773.3 44.8 all-gather.5
  827.2 86.4 reduce-scatter.3
where the time goes:
time: 946 us; the launch traced here: 942 us
  waiting for transfers between devices  360 us (38%)
  blocking collectives  249 us (26%)
  local copies, waits for them, and re-layouts  164 us (17%)
  other arithmetic  97.8 us (10%)
  matrix products  40.8 us (4%)
  between operations  14.9 us (2%)
    psum x1, waiting for transfers between devices, on_device(): query_sum = lax.psum(query_part, 'col')  117 us
    unnamed x7, waiting for transfers between devices  114 us
    add x31, other arithmetic, combine_parts(): rescale(earlier_part[2], factor_one) + rescale(later_part[2], factor_two)  81.3 us
    all_gather x1, waiting for transfers between devices, merged(): pieces = jax.tree.map(lambda part: lax.all_gather(part, axis), value)  76 us
    psum x1, blocking collectives, on_device(): squares = lax.psum(jnp.sum(residual * residual, axis=1), 'col')  62.3 us
    psum x1, blocking collectives, on_device(): squares_two = lax.psum(jnp.sum(middle_wide * middle_wide, axis=1), 'col')  60.6 us
    psum x1, blocking collectives, on_device(): lax.psum(jnp.dot(moe_normed_f, router_weight, precision=lax.Precision.HIG...  60.4 us
    dynamic_slice x62, local copies, waits for them, and re-layouts, merged(): lax.scan(lambda running, slab: (join(running, slab), None), head, tail)  53.9 us
  transfers between devices with their start and end apart: 6, of which 6 were waited for; matrix products, arithmetic and copies ran while one was open for 4% of the time, Pallas kernels for 0%

commit v1 on v0

--- a/solution.py
+++ b/solution.py
@@ -115,7 +115,11 @@
     scale_one = lax.rsqrt(squares / D + norm_epsilon)
     normed = (residual * scale_one[:, None] * attn_gain[None, :]).astype(jnp.bfloat16)
     query_part = jnp.dot(normed, qkv_weight[:, :head_total], preferred_element_type=jnp.float32)
-    query_sum = lax.psum(query_part, "col")
+    query_sum = query_part
+    for hop in (1, 2, 4, 8, 16):
+        query_sum = query_sum + lax.ppermute(
+            query_sum, "col", [(dev, dev ^ hop) for dev in range(32)]
+        )
     queries = (rotate(query_sum, position, HEAD_DIM) * HEAD_DIM ** (-0.5)).astype(jnp.bfloat16)
     key_value = lax.psum_scatter(
         jnp.dot(normed, qkv_weight[:, head_total:], preferred_element_type=jnp.float32).astype(

time: 946 us -> 893 us (0.944)
  waiting for transfers between devices: 360 us -> 294 us
    psum x1 -> x0, waiting for transfers between devices: 117 us -> none  [on_device(): query_sum = lax.psum(query_part, 'col')]
    ppermute x0 -> x5, waiting for transfers between devices: none -> 84.7 us  [on_device(): lax.ppermute(query_sum, 'col', [(dev, dev ^ hop) for dev in range(32)])]
    unnamed x7 -> x6, waiting for transfers between devices: 114 us -> 79.9 us
  transfers between devices with their start and end apart: 6 -> 10, of which waited for: 6 -> 9; matrix products, arithmetic and copies ran while one was open for 4% -> 5% of each run, Pallas kernels for 0% -> 0%
where the time goes in v1:
time: 893 us; the launch traced here: 889 us
  waiting for transfers between devices  294 us (33%)
  blocking collectives  249 us (28%)
  local copies, waits for them, and re-layouts  169 us (19%)
  other arithmetic  101 us (11%)
  matrix products  38.5 us (4%)
  between operations  14.9 us (2%)
  starting transfers between devices  13.2 us (1%)
    ppermute x5, waiting for transfers between devices, on_device(): lax.ppermute(query_sum, 'col', [(dev, dev ^ hop) for dev in range(32)])  84.7 us
    add x31, other arithmetic, combine_parts(): rescale(earlier_part[2], factor_one) + rescale(later_part[2], factor_two)  81.3 us
    unnamed x6, waiting for transfers between devices  79.9 us
    all_gather x1, waiting for transfers between devices, merged(): pieces = jax.tree.map(lambda part: lax.all_gather(part, axis), value)  76.1 us
    psum x1, blocking collectives, on_device(): squares = lax.psum(jnp.sum(residual * residual, axis=1), 'col')  62.3 us
    psum x1, blocking collectives, on_device(): squares_two = lax.psum(jnp.sum(middle_wide * middle_wide, axis=1), 'col')  60.5 us
    psum x1, blocking collectives, on_device(): lax.psum(jnp.dot(moe_normed_f, router_weight, precision=lax.Precision.HIG...  60.4 us
    dynamic_slice x62, local copies, waits for them, and re-layouts, merged(): lax.scan(lambda running, slab: (join(running, slab), None), head, tail)  53.9 us
  transfers between devices with their start and end apart: 10, of which 9 were waited for; matrix products, arithmetic and copies ran while one was open for 5% of the time, Pallas kernels for 0%

profile of v1, /device:TPU:2, one launch (start us, length us, event | category | flops | bytes accessed | tf_op | source)
XLA Modules:
  0.0 889.0 jit_solution(670525164943464244)
XLA Ops:
  8.0 62.3 %psum.21 = f32[128]{0:T(128)S(1)} all-reduce(f32[128]{0:T(128)S(1)} %fusion.64), channel_id=1, replica_groups=mesh['row'=8,'col'=32] {'col'}, use_global_device_ids=true, to_apply=%region_1.2 | all-reduce | flops 128 | bytes 1024 | tf_op jit(solution)/shard_map/psum | solution.py:114
  74.8 5.7 collective-permute-start.1
  80.5 26.3 %collective-permute-done.1 = f32[128,2304]{1,0:T(8,128)S(1)} collective-permute-done((f32[128,2304]{1,0:T(8,128)S(1)}, f32[128,2304]{1,0:T(8,128)S(1)}, u32[]{:S(2)}, u32[]{:S(2)}) %collective-permute-start.1) | collective-permute-done | bytes 1179680 | tf_op jit(solution)/shard_map/ppermute | solution.py:120
  109.5 27.7 %collective-permute-done.2 = f32[128,2304]{1,0:T(8,128)} collective-permute-done((f32[128,2304]{1,0:T(8,128)S(1)}, f32[128,2304]{1,0:T(8,128)}, u32[]{:S(2)}, u32[]{:S(2)}) %collective-permute-start.2) | collective-permute-done | bytes 1179680 | tf_op jit(solution)/shard_map/ppermute | solution.py:120
  139.2 27.9 %collective-permute-done.3 = f32[128,2304]{1,0:T(8,128)} collective-permute-done((f32[128,2304]{1,0:T(8,128)S(1)}, f32[128,2304]{1,0:T(8,128)}, u32[]{:S(2)}, u32[]{:S(2)}) %collective-permute-start.3) | collective-permute-done | bytes 1179680 | tf_op jit(solution)/shard_map/ppermute | solution.py:120
  169.0 7.8 reshape.454
  176.8 6.7 copy.162
  183.5 7.8 reshape.455
  191.3 6.7 copy.163
  199.5 54.5 %all-reduce.3.cloned.1.call-done = bf16[128,4608]{1,0:T(8,128)(2,1)} async-done(((bf16[128,4608]{1,0:T(8,128)(2,1)}), bf16[128,4608]{1,0:T(8,128)(2,1)}) %all-reduce.3.cloned.1.call-update) | async-done | bytes 1179664
  257.5 51.9 %while.31 = (s32[]{:T(128)}, f32[9,4,128]{2,1,0:T(4,128)S(1)}, f32[9,4,128]{2,1,0:T(4,128)S(1)}, f32[9,128,256]{2,1,0:T(8,128)}, s32[9]{0:T(128)S(1)}, /*index=5...) while((s32[]{:T(128)}, f32[9,4,128]{2,1,0:T(4,128)S(1)}, ...), condition=%wide.region_15.16_spmd.clone.clone, body=%wide.region_10.15_spmd.clone.clone.sunk | while | flops 69911040 | bytes 5058339 | solution.py:216
  314.6 24.6 %all-gather = f32[288,4,128]{2,1,0:T(4,128)S(1)} all-gather(f32[9,4,128]{2,1,0:T(4,128)S(1)} %get-tuple-element.105), channel_id=2, replica_groups=mesh['row'=8,'col'=32] {'col'}, dimensions={0}, use_global_device_ids=true | all-gather | bytes 608256 | tf_op jit(solution)/shard_map/all_gather | solution.py:17
  339.3 25.4 %all-gather.1 = f32[288,4,128]{2,1,0:T(4,128)S(1)} all-gather(f32[9,4,128]{2,1,0:T(4,128)S(1)} %get-tuple-element.106), channel_id=3, replica_groups=mesh['row'=8,'col'=32] {'col'}, dimensions={0}, use_global_device_ids=true | all-gather | bytes 608256 | tf_op jit(solution)/shard_map/all_gather | solution.py:17
  364.8 76.1 %all-gather.8.cloned.1.call-done = f32[288,128,256]{2,1,0:T(8,128)} async-done(((f32[9,128,256]{2,1,0:T(8,128)}), f32[288,128,256]{2,1,0:T(8,128)}) %all-gather.8.cloned.1.call-update) | async-done | bytes 37748752 | tf_op jit(solution)/shard_map/all_gather | solution.py:17
  443.6 26.9 %slice.93 = f32[279,128,256]{2,1,0:T(8,128)} slice(f32[288,128,256]{2,1,0:T(8,128)} %all-gather.8.cloned.1.call-done), slice={[9:288], [0:128], [0:256]} | slice | bytes 73138176 | tf_op jit(solution)/shard_map/slice | solution.py:19
  470.5 168.2 %while.30 = (s32[]{:T(128)}, f32[9,4,128]{2,1,0:T(4,128)S(1)}, f32[9,4,128]{2,1,0:T(4,128)S(1)}, f32[9,128,256]{1,2,0:T(8,128)}, f32[31,9,4,128]{3,2,1,0:T(4,128...) while((s32[]{:T(128)}, f32[9,4,128]{2,1,0:T(4,128)S(1)}, ...), condition=%wide.region_17.18_spmd, body=%wide.region_16.17_spmd.sunk | while | flops 916994 | bytes 17676496 | solution.py:20
  641.0 60.5 %psum.22 = f32[128]{0:T(128)S(1)} all-reduce(f32[128]{0:T(128)S(1)} %get-tuple-element.401), channel_id=1, replica_groups=mesh['row'=8,'col'=32] {'col'}, use_global_device_ids=true, to_apply=%region_23.24 | all-reduce | flops 128 | bytes 1024 | tf_op jit(solution)/shard_map/psum | solution.py:228
  703.2 15.9 %all_to_all.14 = bf16[8,64,72]{2,1,0:T(8,128)(2,1)S(1)} all-to-all(bf16[8,64,72]{2,1,0:T(8,128)(2,1)S(1)} %broadcast_select_fusion), channel_id=1, replica_groups=mesh['row'=8,'col'=32] {'row'}, dimensions={0} | all-to-all | bytes 147456 | tf_op jit(solution)/shard_map/all_to_all | solution.py:252
  719.9 44.9 %all-gather.6.cloned.1.call-done = bf16[1,512,2304]{1,2,0:T(8,128)(2,1)} async-done(((bf16[1,512,72]{1,2,0:T(8,128)(2,1)}), bf16[1,512,2304]{1,2,0:T(8,128)(2,1)}) %all-gather.6.cloned.1.call-update) | async-done | bytes 2359312 | tf_op jit(solution)/shard_map/all_gather | solution.py:258
  767.9 3.4 fusion.33
  774.6 60.4 %psum.23 = f32[128,8]{0,1:T(8,128)S(1)} all-reduce(f32[128,8]{0,1:T(8,128)S(1)} %fusion.70), channel_id=1, replica_groups=mesh['row'=8,'col'=32] {'col'}, use_global_device_ids=true, to_apply=%region_26.27 | all-reduce | flops 1024 | bytes 8192 | tf_op jit(solution)/shard_map/psum | solution.py:231
  835.1 25.3 %reduce-scatter.4.cloned.1.call-done = bf16[72,512]{1,0:T(8,128)(2,1)} async-done(((bf16[2304,512]{1,0:T(8,128)(2,1)}), bf16[72,512]{1,0:T(8,128)(2,1)}) %reduce-scatter.4.cloned.1.call-update) | async-done | bytes 73744
  864.5 7.0 all-to-all-start.1
  871.7 8.3 all-to-all-done.1
  (706 shorter events, 253.1 us)
Async XLA Ops:
  7.2 760.7 %copy-start = (bf16[1,180,2304]{2,1,0:T(8,128)(2,1)S(1)}, bf16[1,180,2304]{2,1,0:T(8,128)(2,1)}, u32[]{:S(2)}) copy-start(bf16[1,180,2304]{2,1,0:T(8,128)(2,1)} %param.27) | copy-start | bytes 2488324
  7.2 246.9 %all-reduce.3.cloned.1.call-start = ((), (), s32[]{:S(2)}) async-start(), calls=%async_computation.6 | async-start | bytes 2359296
  71.7 2.9 collective-permute-start
  74.8 32.2 %copy-start.3 = (bf16[72,6912]{1,0:T(8,128)(2,1)S(1)}, bf16[72,6912]{1,0:T(8,128)(2,1)}, u32[]{:S(2)}) copy-start(bf16[72,6912]{1,0:T(8,128)(2,1)} %param.21) | copy-start | bytes 2985988
  74.8 32.2 %copy-start.7 = (bf16[128,72]{0,1:T(8,128)(2,1)S(1)}, bf16[128,72]{0,1:T(8,128)(2,1)}, u32[]{:S(2)}) copy-start(bf16[128,72]{0,1:T(8,128)(2,1)} %param.19) | copy-start | bytes 55300
  74.8 32.2 %copy-start.11 = (f32[72]{0:T(128)S(1)}, f32[72]{0:T(128)}, u32[]{:S(2)}) copy-start(f32[72]{0:T(128)} %param.20) | copy-start | bytes 868
  74.8 31.9 %collective-permute-start.1 = (f32[128,2304]{1,0:T(8,128)S(1)}, f32[128,2304]{1,0:T(8,128)S(1)}, u32[]{:S(2)}, u32[]{:S(2)}) collective-permute-start(f32[128,2304]{1,0:T(8,128)S(1)} %add.210), channel_id=1, source_target_pairs={{0,2},{1,3},{2,0},{3,1},{4,6},{5,7},{6,4},{7,5},{8,10},{9,11},{10,... | collective-permute-start | bytes 3538952 | tf_op jit(solution)/shard_map/ppermute | solution.py:120
  106.9 30.3 %collective-permute-start.2 = (f32[128,2304]{1,0:T(8,128)S(1)}, f32[128,2304]{1,0:T(8,128)}, u32[]{:S(2)}, u32[]{:S(2)}) collective-permute-start(f32[128,2304]{1,0:T(8,128)S(1)} %add.211), channel_id=1, source_target_pairs={{0,4},{1,5},{2,6},{3,7},{4,0},{5,1},{6,2},{7,3},{8,12},{9,13},{10,... | collective-permute-start | bytes 3538952 | tf_op jit(solution)/shard_map/ppermute | solution.py:120
  108.7 332.2 %all-gather.8.cloned.1.call-start = ((), (), s32[]{:S(2)}) async-start(), calls=%async_computation.4 | async-start | bytes 38928384 | tf_op jit(solution)/shard_map/all_gather | solution.py:17
  138.7 28.4 %collective-permute-start.3 = (f32[128,2304]{1,0:T(8,128)S(1)}, f32[128,2304]{1,0:T(8,128)}, u32[]{:S(2)}, u32[]{:S(2)}) collective-permute-start(f32[128,2304]{1,0:T(8,128)S(1)} %add.212), channel_id=1, source_target_pairs={{0,8},{1,9},{2,10},{3,11},{4,12},{5,13},{6,14},{7,15},{8,0},{9,1},... | collective-permute-start | bytes 3538952 | tf_op jit(solution)/shard_map/ppermute | solution.py:120
  168.6 86.7 %collective-permute-start.4 = (f32[128,2304]{1,0:T(8,128)S(1)}, f32[128,2304]{1,0:T(8,128)}, u32[]{:S(2)}, u32[]{:S(2)}) collective-permute-start(f32[128,2304]{1,0:T(8,128)S(1)} %add.213), channel_id=1, source_target_pairs={{0,16},{1,17},{2,18},{3,19},{4,20},{5,21},{6,22},{7,23},{8,24},{9,... | collective-permute-start | bytes 3538952 | tf_op jit(solution)/shard_map/ppermute | solution.py:120
  191.3 6.7 copy-start.17
  309.4 455.4 %all-gather.6.cloned.1.call-start = ((), (), s32[]{:S(2)}) async-start(), calls=%async_computation.3 | async-start | bytes 2433024 | tf_op jit(solution)/shard_map/all_gather | solution.py:258
  473.2 2.6 copy-start.2
  478.7 2.6 copy-start.2
  484.1 2.6 copy-start.2
  489.5 2.6 copy-start.2
  494.9 2.6 copy-start.2
  500.4 2.6 copy-start.2
  549.2 2.6 copy-start.2
  638.7 62.8 %copy-start.12 = (f32[72]{0:T(128)S(1)}, f32[72]{0:T(128)}, u32[]{:S(2)}) copy-start(f32[72]{0:T(128)} %param.23) | copy-start | bytes 868
  641.0 123.9 %copy-start.14 = (bf16[1,2304,180]{1,2,0:T(8,128)(2,1)S(1)}, bf16[1,2304,180]{1,2,0:T(8,128)(2,1)}, u32[]{:S(2)}) copy-start(bf16[1,2304,180]{1,2,0:T(8,128)(2,1)} %param.25) | copy-start | bytes 2488324
  719.8 140.5 %reduce-scatter.4.cloned.1.call-start = ((), (), s32[]{:S(2)}) async-start(), calls=%async_computation.5 | async-start | bytes 2433024
  864.5 15.5 %all-to-all-start.1 = ((bf16[8,2,2304]{2,1,0:T(2,128)(2,1)}), bf16[8,2,2304]{2,1,0:T(2,128)(2,1)S(1)}, u32[]{:S(2)}, u32[]{:S(2)}) async-start(bf16[8,2,2304]{2,1,0:T(2,128)(2,1)} %reshape.465), calls=%async_computation.1 | async-start | bytes 147456 | tf_op jit(solution)/shard_map/all_to_all | solution.py:278
  (125 other events, 212.4 us)
Sparse Core Ops, SparseCore 0:
  108.8 145.1 all-reduce.2
  309.5 131.3 all-gather.7
  720.0 44.8 all-gather.5
  773.9 86.4 reduce-scatter.3
